TPU v7x, 256 devices: a whole 4x4x8 slice. The times are simulated.
256 devices in a mesh: gx: 32 (over x, y, core), gy: 8 (over z).
Axes of the slice: x: 4, y: 4, z: 8, core: 2. Of those that a mesh axis runs over, the one named last changes fastest.
Arguments:
- leaf_load: bfloat16 [65536, 384], P(('gx', 'gy')), may hold values from -6 to 6
- front_zero: bfloat16 [65536, 8192], P(('gx', 'gy')), may hold values from -0.046875 to 0.046875
- front_one: bfloat16 [32768, 8192], P(('gx', 'gy')), may hold values from -0.046875 to 0.046875
- front_two: bfloat16 [16384, 8192], P(('gx', 'gy')), may hold values from -0.046875 to 0.046875
- front_root: bfloat16 [8192, 8192], P(('gx', 'gy')), may hold values from -0.046875 to 0.046875
- load_one: float32 [32768, 384], P(('gx', 'gy')), may hold values from -6 to 6
- load_two: float32 [16384, 384], P(('gx', 'gy')), may hold values from -6 to 6
- load_root: float32 [8192, 384], P(('gx', 'gy')), may hold values from -6 to 6
- map_one: int32 [8192, 2], replicated, may hold values from 0 to 255
- map_two: int32 [8192, 2], replicated, may hold values from 0 to 127
- map_root: int32 [8192, 2], replicated, may hold values from 0 to 63
- adjoint: float32 [64, 128, 384], P('gx', 'gy'), may hold values from -6 to 6
Outputs:
- root_solution: float32 [8192, 384], P(('gx', 'gy'))
- gradient: float32 [64, 128, 384], P('gx', 'gy')
All inputs are finite; a program needn't handle non-finite values.
Results may differ from a plain program's by a relative error of at most 0.0055.
Values may be sent and summed in bfloat16 or wider, within the bound.
No kernel may reach another device: no remote copies, remote signals or barrier semaphores. Data moves between devices by JAX's collectives and lax.ppermute only.
A program may use at most 64 MiB of HBM per device.

v0:
```python
import jax
import jax.numpy as jnp
from jax import lax
from jax.sharding import PartitionSpec as P


def swapped(x, axis, distance):
    return lax.ppermute(x, axis, [(i, i ^ 1 << distance) for i in range(lax.axis_size(axis))])


def padded_2(cells, sides, width):
    for axis, dim in sides:
        count = lax.axis_size(axis)
        ends = count - 1
        head = lax.slice_in_dim(cells, 0, width, axis=dim)
        tail = lax.slice_in_dim(cells, cells.shape[dim] - width, cells.shape[dim], axis=dim)
        cells = jnp.concatenate(
            [
                lax.ppermute(tail, axis, [(i, (i + 1) % count) for i in range(ends)]),
                cells,
                lax.ppermute(head, axis, [((i + 1) % count, i) for i in range(ends)]),
            ],
            axis=dim,
        )
    return cells


def group_rows(values, bits):
    values = lax.all_gather(values, "gy", axis=0, tiled=True)
    column = lax.axis_index("gx")
    for bit in range(bits):
        other = swapped(values, "gx", bit)
        upper = column >> bit & 1 == 1
        values = jnp.where(
            upper, jnp.concatenate([other, values], 0), jnp.concatenate([values, other], 0)
        )
    return values


def local(
    leaf_load,
    front_zero,
    front_one,
    front_two,
    front_root,
    load_one,
    load_two,
    load_root,
    map_one,
    map_two,
    map_root,
    adjoint,
):
    leaf_bits = lax.axis_size("gx").bit_length() - 4
    fronts = (front_zero, front_one, front_two)
    loads = (load_one, load_two, load_root)
    mappings = (map_one, map_two, map_root)
    column = lax.axis_index("gx")
    row_index = lax.axis_index("gy")
    state = leaf_load
    for level in range(3):
        bits = leaf_bits + level
        whole = group_rows(state, bits)
        product = jnp.dot(fronts[level], whole, preferred_element_type=jnp.float32)
        other = swapped(product, "gx", bits)
        upper = column >> bits & 1 == 1
        first = jnp.where(upper, other, product)
        second = jnp.where(upper, product, other)
        half = product.shape[0] // 2
        position = column % 2 ** (bits + 1) * lax.axis_size("gy") + row_index
        local_map = lax.dynamic_slice_in_dim(mappings[level], position * half, half, 0)
        total = (
            loads[level]
            + jnp.take(first, local_map[:, 0], axis=0)
            + jnp.take(second, local_map[:, 1], axis=0)
        )
        state = total.astype(jnp.bfloat16)
    whole = group_rows(state, leaf_bits + 3)
    root_solution = jnp.dot(front_root, whole, preferred_element_type=jnp.float32)
    cells_x = adjoint.shape[0]
    cells_y = adjoint.shape[1]
    width = adjoint.shape[2]
    plane = root_solution.reshape(cells_x, cells_y, width)
    stacked = jnp.stack([plane, adjoint])
    padded = padded_2(stacked, (("gx", 1), ("gy", 2)), 1)
    padded_u = padded[0]
    padded_a = padded[1]
    gradient = jnp.zeros((cells_x, cells_y, width), jnp.float32)
    for lo_x, lo_y in ((2, 1), (0, 1), (1, 2), (1, 0)):
        near_u = padded_u[lo_x : lo_x + cells_x, lo_y : lo_y + cells_y]
        near_a = padded_a[lo_x : lo_x + cells_x, lo_y : lo_y + cells_y]
        gradient = gradient + (plane - near_u) * (adjoint - near_a)
    return (root_solution, gradient)


def solution(mesh):
    in_specs = (
        P(("gx", "gy"), None),
        P(("gx", "gy"), None),
        P(("gx", "gy"), None),
        P(("gx", "gy"), None),
        P(("gx", "gy"), None),
        P(("gx", "gy"), None),
        P(("gx", "gy"), None),
        P(("gx", "gy"), None),
        P(),
        P(),
        P(),
        P("gx", "gy", None),
    )
    out_specs = (P(("gx", "gy"), None), P("gx", "gy", None))
    return jax.shard_map(local, mesh=mesh, in_specs=in_specs, out_specs=out_specs, check_vma=False)
```

profile of v0, /device:TPU:34, one launch (start us, length us, event | category | flops | bytes accessed | tf_op | source)
XLA Modules:
  0.0 686.3 jit_solution(2727871176709467057)
XLA Ops:
  7.9 44.2 %all-gather.2.cloned.1.call-done = bf16[2048,384]{1,0:T(8,128)(2,1)} async-done(((bf16[256,384]{1,0:T(8,128)(2,1)}), bf16[2048,384]{1,0:T(8,128)(2,1)}) %all-gather.2.cloned.1.call-update) | async-done | bytes 1572880 | tf_op jit(solution)/shard_map/all_gather | solution.py:29
  55.8 5.5 maximum_select_fusion.8
  62.8 69.0 %collective-permute-done.1 = bf16[4096,384]{1,0:T(8,128)(2,1)} collective-permute-done((bf16[4096,384]{1,0:T(8,128)(2,1)}, bf16[4096,384]{1,0:T(8,128)(2,1)}, u32[]{:S(2)}, u32[]{:S(2)}) %collective-permute-start.1) | collective-permute-done | bytes 3145760 | tf_op jit(solution)/shard_map/ppermute | solution.py:8
  131.8 9.1 %fusion.28 = f32[256,384]{0,1:T(8,128)S(1)} fusion(bf16[256,8192]{1,0:T(8,128)(2,1)} %param.19, bf16[4096,384]{1,0:T(8,128)(2,1)} %maximum_select_fusion.8, bf16[4096,384]{1,0:T(8,128)(2,1)} %collective-permute-done.1, pred[]{:T(512)S(6)} %eq.17), kind=kOutput, calls=%fused_computation.45 | convolution fusion | flops 1638924288 | bytes 10878977 | tf_op jit(solution)/shard_map/dot_general | solution.py:64
  144.7 8.1 %collective-permute-done.2 = f32[256,384]{0,1:T(8,128)S(1)} collective-permute-done((f32[256,384]{0,1:T(8,128)S(1)}, f32[256,384]{0,1:T(8,128)S(1)}, u32[]{:S(2)}, u32[]{:S(2)}) %collective-permute-start.2) | collective-permute-done | bytes 393248 | tf_op jit(solution)/shard_map/ppermute | solution.py:8
  154.8 25.7 %all_gather.13 = bf16[1024,384]{1,0:T(8,128)(2,1)S(1)} all-gather(bf16[128,384]{1,0:T(8,128)(2,1)S(1)} %fusion.31), channel_id=1, replica_groups=mesh['gx'=32,'gy'=8] {'gy'}, dimensions={0}, use_global_device_ids=true | all-gather | bytes 884736 | tf_op jit(solution)/shard_map/all_gather | solution.py:29
  184.8 35.0 %collective-permute-done.4 = bf16[2048,384]{1,0:T(8,128)(2,1)S(1)} collective-permute-done((bf16[2048,384]{1,0:T(8,128)(2,1)S(1)}, bf16[2048,384]{1,0:T(8,128)(2,1)S(1)}, u32[]{:S(2)}, u32[]{:S(2)}) %collective-permute-start.4) | collective-permute-done | bytes 1572896 | tf_op jit(solution)/shard_map/ppermute | solution.py:8
  219.8 8.3 %maximum_select_fusion.9 = bf16[4096,384]{1,0:T(8,128)(2,1)} fusion(bf16[2048,384]{1,0:T(8,128)(2,1)S(1)} %maximum_select_fusion.12, bf16[2048,384]{1,0:T(8,128)(2,1)S(1)} %collective-permute-done.4, pred[]{:T(512)S(6)} %eq.17), kind=kLoop, calls=%fused_computation.39 | loop fusion | flops 14155776 | bytes 6291457 | tf_op jit(solution)/shard_map/jit(_where)/select_n | solution.py:34
  231.8 67.4 %collective-permute-done.5 = bf16[4096,384]{1,0:T(8,128)(2,1)} collective-permute-done((bf16[4096,384]{1,0:T(8,128)(2,1)}, bf16[4096,384]{1,0:T(8,128)(2,1)}, u32[]{:S(2)}, u32[]{:S(2)}) %collective-permute-start.5) | collective-permute-done | bytes 3145760 | tf_op jit(solution)/shard_map/ppermute | solution.py:8
  299.2 6.3 fusion.29
  306.4 5.1 collective-permute-done.6
  313.2 25.2 %all_gather.14 = bf16[512,384]{1,0:T(8,128)(2,1)S(1)} all-gather(bf16[64,384]{1,0:T(8,128)(2,1)S(1)} %fusion.32), channel_id=1, replica_groups=mesh['gx'=32,'gy'=8] {'gy'}, dimensions={0}, use_global_device_ids=true | all-gather | bytes 442368 | tf_op jit(solution)/shard_map/all_gather | solution.py:29
  342.0 18.1 %collective-permute-done.8 = bf16[1024,384]{1,0:T(8,128)(2,1)S(1)} collective-permute-done((bf16[1024,384]{1,0:T(8,128)(2,1)S(1)}, bf16[1024,384]{1,0:T(8,128)(2,1)S(1)}, u32[]{:S(2)}, u32[]{:S(2)}) %collective-permute-start.8) | collective-permute-done | bytes 786464 | tf_op jit(solution)/shard_map/ppermute | solution.py:8
  363.6 34.1 %collective-permute-done.9 = bf16[2048,384]{1,0:T(8,128)(2,1)S(1)} collective-permute-done((bf16[2048,384]{1,0:T(8,128)(2,1)S(1)}, bf16[2048,384]{1,0:T(8,128)(2,1)S(1)}, u32[]{:S(2)}, u32[]{:S(2)}) %collective-permute-start.9) | collective-permute-done | bytes 1572896 | tf_op jit(solution)/shard_map/ppermute | solution.py:8
  397.7 8.3 %maximum_select_fusion.10 = bf16[4096,384]{1,0:T(8,128)(2,1)} fusion(bf16[2048,384]{1,0:T(8,128)(2,1)S(1)} %maximum_select_fusion.13, bf16[2048,384]{1,0:T(8,128)(2,1)S(1)} %collective-permute-done.9, pred[]{:T(512)S(6)} %eq.16), kind=kLoop, calls=%fused_computation.40 | loop fusion | flops 14155776 | bytes 6291457 | tf_op jit(solution)/shard_map/jit(_where)/select_n | solution.py:34
  407.3 67.4 %collective-permute-done.10 = bf16[4096,384]{1,0:T(8,128)(2,1)} collective-permute-done((bf16[4096,384]{1,0:T(8,128)(2,1)}, bf16[4096,384]{1,0:T(8,128)(2,1)}, u32[]{:S(2)}, u32[]{:S(2)}) %collective-permute-start.10) | collective-permute-done | bytes 3145760 | tf_op jit(solution)/shard_map/ppermute | solution.py:8
  474.7 6.2 fusion.30
  488.5 24.8 %all_gather.15 = bf16[256,384]{1,0:T(8,128)(2,1)S(1)} all-gather(bf16[32,384]{1,0:T(8,128)(2,1)S(1)} %fusion.41), channel_id=1, replica_groups=mesh['gx'=32,'gy'=8] {'gy'}, dimensions={0}, use_global_device_ids=true | all-gather | bytes 221184 | tf_op jit(solution)/shard_map/all_gather | solution.py:29
  516.4 9.7 %collective-permute-done.13 = bf16[512,384]{1,0:T(8,128)(2,1)S(1)} collective-permute-done((bf16[512,384]{1,0:T(8,128)(2,1)S(1)}, bf16[512,384]{1,0:T(8,128)(2,1)S(1)}, u32[]{:S(2)}, u32[]{:S(2)}) %collective-permute-start.13) | collective-permute-done | bytes 393248 | tf_op jit(solution)/shard_map/ppermute | solution.py:8
  529.5 17.2 %collective-permute-done.14 = bf16[1024,384]{1,0:T(8,128)(2,1)S(1)} collective-permute-done((bf16[1024,384]{1,0:T(8,128)(2,1)S(1)}, bf16[1024,384]{1,0:T(8,128)(2,1)S(1)}, u32[]{:S(2)}, u32[]{:S(2)}) %collective-permute-start.14) | collective-permute-done | bytes 786464 | tf_op jit(solution)/shard_map/ppermute | solution.py:8
  548.1 34.1 %collective-permute-done.15 = bf16[2048,384]{1,0:T(8,128)(2,1)S(1)} collective-permute-done((bf16[2048,384]{1,0:T(8,128)(2,1)S(1)}, bf16[2048,384]{1,0:T(8,128)(2,1)S(1)}, u32[]{:S(2)}, u32[]{:S(2)}) %collective-permute-start.15) | collective-permute-done | bytes 1572896 | tf_op jit(solution)/shard_map/ppermute | solution.py:8
  582.2 7.2 %maximum_select_fusion.11 = bf16[4096,384]{1,0:T(8,128)(2,1)S(1)} fusion(bf16[2048,384]{1,0:T(8,128)(2,1)S(1)} %maximum_select_fusion.14, bf16[2048,384]{1,0:T(8,128)(2,1)S(1)} %collective-permute-done.15, pred[]{:T(512)S(6)} %eq.15), kind=kLoop, calls=%fused_computation.41 | loop fusion | flops 14155776 | bytes 6291457 | tf_op jit(solution)/shard_map/jit(_where)/select_n | solution.py:34
  591.6 66.9 %collective-permute-done.16 = bf16[4096,384]{1,0:T(8,128)(2,1)S(1)} collective-permute-done((bf16[4096,384]{1,0:T(8,128)(2,1)S(1)}, bf16[4096,384]{1,0:T(8,128)(2,1)S(1)}, u32[]{:S(2)}, u32[]{:S(2)}) %collective-permute-start.16) | collective-permute-done | bytes 3145760 | tf_op jit(solution)/shard_map/ppermute | solution.py:8
  664.7 5.1 collective-permute-done.17
  (84 shorter events, 64.1 us)
Async XLA Ops:
  7.2 292.0 %copy-start = (bf16[128,8192]{1,0:T(8,128)(2,1)S(1)}, bf16[128,8192]{1,0:T(8,128)(2,1)}, u32[]{:S(2)}) copy-start(bf16[128,8192]{1,0:T(8,128)(2,1)} %param.20) | copy-start | bytes 6291460
  7.2 44.9 %all-gather.2.cloned.1.call-start = ((), (), s32[]{:S(2)}) async-start(), calls=%async_computation | async-start | bytes 1769472 | tf_op jit(solution)/shard_map/all_gather | solution.py:29
  52.1 3.8 collective-permute-start
  61.3 70.5 %collective-permute-start.1 = (bf16[4096,384]{1,0:T(8,128)(2,1)}, bf16[4096,384]{1,0:T(8,128)(2,1)}, u32[]{:S(2)}, u32[]{:S(2)}) collective-permute-start(bf16[4096,384]{1,0:T(8,128)(2,1)} %maximum_select_fusion.8), channel_id=1, source_target_pairs={{0,16},{8,24},{16,0},{24,8},{32,48},{40,56},{48,32},{56,40},{64,80... | collective-permute-start | bytes 9437192 | tf_op jit(solution)/shard_map/ppermute | solution.py:8
  140.8 11.9 %collective-permute-start.2 = (f32[256,384]{0,1:T(8,128)S(1)}, f32[256,384]{0,1:T(8,128)S(1)}, u32[]{:S(2)}, u32[]{:S(2)}) collective-permute-start(f32[256,384]{0,1:T(8,128)S(1)} %fusion.28), channel_id=1, source_target_pairs={{0,32},{8,40},{16,48},{24,56},{32,0},{40,8},{48,16},{56,24},{64,96... | collective-permute-start | bytes 1179656 | tf_op jit(solution)/shard_map/ppermute | solution.py:8
  180.5 2.3 collective-permute-start.3
  183.2 36.5 %collective-permute-start.4 = (bf16[2048,384]{1,0:T(8,128)(2,1)S(1)}, bf16[2048,384]{1,0:T(8,128)(2,1)S(1)}, u32[]{:S(2)}, u32[]{:S(2)}) collective-permute-start(bf16[2048,384]{1,0:T(8,128)(2,1)S(1)} %maximum_select_fusion.12), channel_id=1, source_target_pairs={{0,16},{8,24},{16,0},{24,8},{32,48},{40,56},{48,32},{56,40},{64,80... | collective-permute-start | bytes 4718600 | tf_op jit(solution)/shard_map/ppermute | solution.py:8
  228.0 71.1 %collective-permute-start.5 = (bf16[4096,384]{1,0:T(8,128)(2,1)}, bf16[4096,384]{1,0:T(8,128)(2,1)}, u32[]{:S(2)}, u32[]{:S(2)}) collective-permute-start(bf16[4096,384]{1,0:T(8,128)(2,1)} %maximum_select_fusion.9), channel_id=1, source_target_pairs={{0,32},{8,40},{16,48},{24,56},{32,0},{40,8},{48,16},{56,24},{64,96... | collective-permute-start | bytes 9437192 | tf_op jit(solution)/shard_map/ppermute | solution.py:8
  305.5 5.9 collective-permute-start.6
  338.4 1.7 collective-permute-start.7
  340.4 19.7 %collective-permute-start.8 = (bf16[1024,384]{1,0:T(8,128)(2,1)S(1)}, bf16[1024,384]{1,0:T(8,128)(2,1)S(1)}, u32[]{:S(2)}, u32[]{:S(2)}) collective-permute-start(bf16[1024,384]{1,0:T(8,128)(2,1)S(1)} %maximum_select_fusion.21), channel_id=1, source_target_pairs={{0,16},{8,24},{16,0},{24,8},{32,48},{40,56},{48,32},{56,40},{64,80... | collective-permute-start | bytes 2359304 | tf_op jit(solution)/shard_map/ppermute | solution.py:8
  360.5 114.2 %copy-start.6 = (bf16[64,8192]{1,0:T(8,128)(2,1)S(1)}, bf16[64,8192]{1,0:T(8,128)(2,1)}, u32[]{:S(2)}) copy-start(bf16[64,8192]{1,0:T(8,128)(2,1)} %param.21) | copy-start | bytes 3145732
  360.5 37.2 %collective-permute-start.9 = (bf16[2048,384]{1,0:T(8,128)(2,1)S(1)}, bf16[2048,384]{1,0:T(8,128)(2,1)S(1)}, u32[]{:S(2)}, u32[]{:S(2)}) collective-permute-start(bf16[2048,384]{1,0:T(8,128)(2,1)S(1)} %maximum_select_fusion.13), channel_id=1, source_target_pairs={{0,32},{8,40},{16,48},{24,56},{32,0},{40,8},{48,16},{56,24},{64,96... | collective-permute-start | bytes 4718600 | tf_op jit(solution)/shard_map/ppermute | solution.py:8
  406.0 68.7 %collective-permute-start.10 = (bf16[4096,384]{1,0:T(8,128)(2,1)}, bf16[4096,384]{1,0:T(8,128)(2,1)}, u32[]{:S(2)}, u32[]{:S(2)}) collective-permute-start(bf16[4096,384]{1,0:T(8,128)(2,1)} %maximum_select_fusion.10), channel_id=1, source_target_pairs={{0,64},{8,72},{16,80},{24,88},{32,96},{40,104},{48,112},{56,120},{... | collective-permute-start | bytes 9437192 | tf_op jit(solution)/shard_map/ppermute | solution.py:8
  480.9 6.2 collective-permute-start.11
  513.3 1.4 collective-permute-start.12
  514.9 11.2 %collective-permute-start.13 = (bf16[512,384]{1,0:T(8,128)(2,1)S(1)}, bf16[512,384]{1,0:T(8,128)(2,1)S(1)}, u32[]{:S(2)}, u32[]{:S(2)}) collective-permute-start(bf16[512,384]{1,0:T(8,128)(2,1)S(1)} %maximum_select_fusion.23), channel_id=1, source_target_pairs={{0,16},{8,24},{16,0},{24,8},{32,48},{40,56},{48,32},{56,40},{64,80... | collective-permute-start | bytes 1179656 | tf_op jit(solution)/shard_map/ppermute | solution.py:8
  526.4 20.3 %collective-permute-start.14 = (bf16[1024,384]{1,0:T(8,128)(2,1)S(1)}, bf16[1024,384]{1,0:T(8,128)(2,1)S(1)}, u32[]{:S(2)}, u32[]{:S(2)}) collective-permute-start(bf16[1024,384]{1,0:T(8,128)(2,1)S(1)} %maximum_select_fusion.22), channel_id=1, source_target_pairs={{0,32},{8,40},{16,48},{24,56},{32,0},{40,8},{48,16},{56,24},{64,96... | collective-permute-start | bytes 2359304 | tf_op jit(solution)/shard_map/ppermute | solution.py:8
  547.2 35.0 %collective-permute-start.15 = (bf16[2048,384]{1,0:T(8,128)(2,1)S(1)}, bf16[2048,384]{1,0:T(8,128)(2,1)S(1)}, u32[]{:S(2)}, u32[]{:S(2)}) collective-permute-start(bf16[2048,384]{1,0:T(8,128)(2,1)S(1)} %maximum_select_fusion.14), channel_id=1, source_target_pairs={{0,64},{8,72},{16,80},{24,88},{32,96},{40,104},{48,112},{56,120},{... | collective-permute-start | bytes 4718600 | tf_op jit(solution)/shard_map/ppermute | solution.py:8
  589.4 69.1 %collective-permute-start.16 = (bf16[4096,384]{1,0:T(8,128)(2,1)S(1)}, bf16[4096,384]{1,0:T(8,128)(2,1)S(1)}, u32[]{:S(2)}, u32[]{:S(2)}) collective-permute-start(bf16[4096,384]{1,0:T(8,128)(2,1)S(1)} %maximum_select_fusion.11), channel_id=1, source_target_pairs={{0,128},{8,136},{16,144},{24,152},{32,160},{40,168},{48,176},{56,1... | collective-permute-start | bytes 9437192 | tf_op jit(solution)/shard_map/ppermute | solution.py:8
  660.3 4.3 collective-permute-start.18
  662.3 7.5 %collective-permute-start.17 = (f32[2,1,16,384]{3,2,1,0:T(8,128)S(1)}, f32[2,1,16,384]{3,2,1,0:T(8,128)S(1)}, u32[]{:S(2)}, u32[]{:S(2)}) collective-permute-start(f32[2,1,16,384]{3,2,1,0:T(8,128)S(1)} %get-tuple-element.27), channel_id=1, source_target_pairs={{0,8},{8,16},{16,24},{24,32},{32,40},{40,48},{48,56},{56,64},{64,7... | collective-permute-start | bytes 147464 | tf_op jit(solution)/shard_map/ppermute | solution.py:19
  669.8 5.9 collective-permute-start.20
  673.1 5.6 collective-permute-start.19
  (6 other events, 300.0 us)
Sparse Core Ops, SparseCore 0:
  9.8 42.2 all-gather.1
where the time goes:
time: 687 us; the launch traced here: 686 us
  waiting for transfers between devices  498 us (72%)
  blocking collectives  75.7 us (11%)
  starting transfers between devices  35.3 us (5%)
  other arithmetic  32.4 us (5%)
  matrix products  23.4 us (3%)
  between operations  14.4 us (2%)
  local copies, waits for them, and re-layouts  6.91 us (1%)
    ppermute x17, waiting for transfers between devices, swapped(): lax.ppermute(x, axis, [(i, i ^ 1 << distance) for i in range(lax.axis_siz...  445 us
    all_gather x3, blocking collectives, group_rows(): values = lax.all_gather(values, 'gy', axis=0, tiled=True)  75.7 us
    all_gather x1, waiting for transfers between devices, group_rows(): values = lax.all_gather(values, 'gy', axis=0, tiled=True)  44.2 us
    select_n x10, other arithmetic, group_rows(): jnp.where(upper, jnp.concatenate([other, values], 0), jnp.concatenate([va...  31.2 us
    ppermute x17, starting transfers between devices, swapped(): lax.ppermute(x, axis, [(i, i ^ 1 << distance) for i in range(lax.axis_siz...  25.1 us
    dot_general x3, matrix products, local(): product = jnp.dot(fronts[level], whole, preferred_element_type=jnp.float32)  21.6 us
  transfers between devices with their start and end apart: 22, of which 20 were waited for; matrix products, arithmetic and copies ran while one was open for 0% of the time, Pallas kernels for 0%

commit v1 on v0

--- a/solution.py
+++ b/solution.py
@@ -26,7 +26,10 @@
 
 
 def group_rows(values, bits):
-    values = lax.all_gather(values, "gy", axis=0, tiled=True)
+    size = lax.axis_size("gy")
+    parts = jnp.stack([values for _ in range(size)])
+    parts = lax.all_to_all(parts, "gy", split_axis=0, concat_axis=0)
+    values = jnp.concatenate(parts, axis=0)
     column = lax.axis_index("gx")
     for bit in range(bits):
         other = swapped(values, "gx", bit)

time: 687 us -> 652 us (0.949)
  waiting for transfers between devices: 498 us -> 452 us
  blocking collectives: 75.7 us -> 98.3 us
  between operations: 14.4 us -> 1 us
    all_to_all x0 -> x4, blocking collectives: none -> 98.3 us  [group_rows(): parts = lax.all_to_all(parts, 'gy', split_axis=0, concat_axis=0)]
    all_gather x3 -> x0, blocking collectives: 75.7 us -> none  [group_rows(): values = lax.all_gather(values, 'gy', axis=0, tiled=True)]
    all_gather x1 -> x0, waiting for transfers between devices: 44.2 us -> none  [group_rows(): values = lax.all_gather(values, 'gy', axis=0, tiled=True)]
  transfers between devices with their start and end apart: 22 -> 21, of which waited for: 20 -> 19; matrix products, arithmetic and copies ran while one was open for 0% -> 0% of each run, Pallas kernels for 0% -> 0%
where the time goes in v1:
time: 652 us
  waiting for transfers between devices  452 us (69%)
  blocking collectives  98.3 us (15%)
  starting transfers between devices  36.3 us (6%)
  other arithmetic  32.3 us (5%)
  matrix products  23.3 us (4%)
  local copies, waits for them, and re-layouts  8.24 us (1%)
    ppermute x17, waiting for transfers between devices, swapped(): lax.ppermute(x, axis, [(i, i ^ 1 << distance) for i in range(lax.axis_siz...  444 us
    all_to_all x4, blocking collectives, group_rows(): parts = lax.all_to_all(parts, 'gy', split_axis=0, concat_axis=0)  98.3 us
    select_n x10, other arithmetic, group_rows(): jnp.where(upper, jnp.concatenate([other, values], 0), jnp.concatenate([va...  31.1 us
    ppermute x17, starting transfers between devices, swapped(): lax.ppermute(x, axis, [(i, i ^ 1 << distance) for i in range(lax.axis_siz...  26.2 us
    dot_general x3, matrix products, local(): product = jnp.dot(fronts[level], whole, preferred_element_type=jnp.float32)  21.5 us
  transfers between devices with their start and end apart: 21, of which 19 were waited for; matrix products, arithmetic and copies ran while one was open for 0% of the time, Pallas kernels for 0%

profile of v1, /device:TPU:34, one launch (start us, length us, event | category | flops | bytes accessed | tf_op | source)
XLA Modules:
  0.0 651.8 jit_solution(12825064988890354405)
XLA Ops:
  1.9 47.0 %all_to_all.20 = bf16[8,256,384]{2,1,0:T(8,128)(2,1)} all-to-all(bf16[8,256,384]{2,1,0:T(8,128)(2,1)S(1)} %stack.12), channel_id=1, replica_groups=mesh['gx'=32,'gy'=8] {'gy'}, dimensions={0} | all-to-all | bytes 3145728 | tf_op jit(solution)/shard_map/all_to_all | solution.py:31
  52.6 5.4 maximum_select_fusion.8
  59.6 68.9 %collective-permute-done.1 = bf16[4096,384]{1,0:T(8,128)(2,1)} collective-permute-done((bf16[4096,384]{1,0:T(8,128)(2,1)}, bf16[4096,384]{1,0:T(8,128)(2,1)}, u32[]{:S(2)}, u32[]{:S(2)}) %collective-permute-start.1) | collective-permute-done | bytes 3145760 | tf_op jit(solution)/shard_map/ppermute | solution.py:8
  128.5 9.0 %fusion.28 = f32[256,384]{0,1:T(8,128)S(1)} fusion(bf16[256,8192]{1,0:T(8,128)(2,1)} %param.19, bf16[4096,384]{1,0:T(8,128)(2,1)} %maximum_select_fusion.8, bf16[4096,384]{1,0:T(8,128)(2,1)} %collective-permute-done.1, pred[]{:T(512)S(6)} %eq.17), kind=kOutput, calls=%fused_computation.45 | convolution fusion | flops 1638924288 | bytes 10878977 | tf_op jit(solution)/shard_map/dot_general | solution.py:67
  141.5 7.9 %collective-permute-done.2 = f32[256,384]{0,1:T(8,128)S(1)} collective-permute-done((f32[256,384]{0,1:T(8,128)S(1)}, f32[256,384]{0,1:T(8,128)S(1)}, u32[]{:S(2)}, u32[]{:S(2)}) %collective-permute-start.2) | collective-permute-done | bytes 393248 | tf_op jit(solution)/shard_map/ppermute | solution.py:8
  151.6 24.4 %all_to_all.21 = bf16[8,128,384]{2,1,0:T(8,128)(2,1)S(1)} all-to-all(bf16[8,128,384]{2,1,0:T(8,128)(2,1)S(1)} %stack.13), channel_id=1, replica_groups=mesh['gx'=32,'gy'=8] {'gy'}, dimensions={0} | all-to-all | bytes 1572864 | tf_op jit(solution)/shard_map/all_to_all | solution.py:31
  180.3 34.9 %collective-permute-done.4 = bf16[2048,384]{1,0:T(8,128)(2,1)S(1)} collective-permute-done((bf16[2048,384]{1,0:T(8,128)(2,1)S(1)}, bf16[2048,384]{1,0:T(8,128)(2,1)S(1)}, u32[]{:S(2)}, u32[]{:S(2)}) %collective-permute-start.4) | collective-permute-done | bytes 1572896 | tf_op jit(solution)/shard_map/ppermute | solution.py:8
  215.2 8.2 %maximum_select_fusion.9 = bf16[4096,384]{1,0:T(8,128)(2,1)} fusion(bf16[2048,384]{1,0:T(8,128)(2,1)S(1)} %maximum_select_fusion.12, bf16[2048,384]{1,0:T(8,128)(2,1)S(1)} %collective-permute-done.4, pred[]{:T(512)S(6)} %eq.17), kind=kLoop, calls=%fused_computation.39 | loop fusion | flops 14155776 | bytes 6291457 | tf_op jit(solution)/shard_map/jit(_where)/select_n | solution.py:37
  227.3 67.2 %collective-permute-done.5 = bf16[4096,384]{1,0:T(8,128)(2,1)} collective-permute-done((bf16[4096,384]{1,0:T(8,128)(2,1)}, bf16[4096,384]{1,0:T(8,128)(2,1)}, u32[]{:S(2)}, u32[]{:S(2)}) %collective-permute-start.5) | collective-permute-done | bytes 3145760 | tf_op jit(solution)/shard_map/ppermute | solution.py:8
  294.5 6.3 fusion.29
  301.7 5.1 collective-permute-done.6
  308.6 14.6 %all_to_all.22 = bf16[8,64,384]{2,1,0:T(8,128)(2,1)S(1)} all-to-all(bf16[8,64,384]{2,1,0:T(8,128)(2,1)S(1)} %stack.14), channel_id=1, replica_groups=mesh['gx'=32,'gy'=8] {'gy'}, dimensions={0} | all-to-all | bytes 786432 | tf_op jit(solution)/shard_map/all_to_all | solution.py:31
  326.8 18.0 %collective-permute-done.8 = bf16[1024,384]{1,0:T(8,128)(2,1)S(1)} collective-permute-done((bf16[1024,384]{1,0:T(8,128)(2,1)S(1)}, bf16[1024,384]{1,0:T(8,128)(2,1)S(1)}, u32[]{:S(2)}, u32[]{:S(2)}) %collective-permute-start.8) | collective-permute-done | bytes 786464 | tf_op jit(solution)/shard_map/ppermute | solution.py:8
  348.6 33.9 %collective-permute-done.9 = bf16[2048,384]{1,0:T(8,128)(2,1)S(1)} collective-permute-done((bf16[2048,384]{1,0:T(8,128)(2,1)S(1)}, bf16[2048,384]{1,0:T(8,128)(2,1)S(1)}, u32[]{:S(2)}, u32[]{:S(2)}) %collective-permute-start.9) | collective-permute-done | bytes 1572896 | tf_op jit(solution)/shard_map/ppermute | solution.py:8
  382.5 8.2 %maximum_select_fusion.10 = bf16[4096,384]{1,0:T(8,128)(2,1)} fusion(bf16[2048,384]{1,0:T(8,128)(2,1)S(1)} %maximum_select_fusion.13, bf16[2048,384]{1,0:T(8,128)(2,1)S(1)} %collective-permute-done.9, pred[]{:T(512)S(6)} %eq.16), kind=kLoop, calls=%fused_computation.40 | loop fusion | flops 14155776 | bytes 6291457 | tf_op jit(solution)/shard_map/jit(_where)/select_n | solution.py:37
  392.0 67.4 %collective-permute-done.10 = bf16[4096,384]{1,0:T(8,128)(2,1)} collective-permute-done((bf16[4096,384]{1,0:T(8,128)(2,1)}, bf16[4096,384]{1,0:T(8,128)(2,1)}, u32[]{:S(2)}, u32[]{:S(2)}) %collective-permute-start.10) | collective-permute-done | bytes 3145760 | tf_op jit(solution)/shard_map/ppermute | solution.py:8
  459.5 6.2 fusion.30
  473.2 12.4 %all_to_all.23 = bf16[8,32,384]{2,1,0:T(8,128)(2,1)S(1)} all-to-all(bf16[8,32,384]{2,1,0:T(8,128)(2,1)S(1)} %stack.15), channel_id=1, replica_groups=mesh['gx'=32,'gy'=8] {'gy'}, dimensions={0} | all-to-all | bytes 393216 | tf_op jit(solution)/shard_map/all_to_all | solution.py:31
  488.8 9.6 %collective-permute-done.13 = bf16[512,384]{1,0:T(8,128)(2,1)S(1)} collective-permute-done((bf16[512,384]{1,0:T(8,128)(2,1)S(1)}, bf16[512,384]{1,0:T(8,128)(2,1)S(1)}, u32[]{:S(2)}, u32[]{:S(2)}) %collective-permute-start.13) | collective-permute-done | bytes 393248 | tf_op jit(solution)/shard_map/ppermute | solution.py:8
  502.0 17.1 %collective-permute-done.14 = bf16[1024,384]{1,0:T(8,128)(2,1)S(1)} collective-permute-done((bf16[1024,384]{1,0:T(8,128)(2,1)S(1)}, bf16[1024,384]{1,0:T(8,128)(2,1)S(1)}, u32[]{:S(2)}, u32[]{:S(2)}) %collective-permute-start.14) | collective-permute-done | bytes 786464 | tf_op jit(solution)/shard_map/ppermute | solution.py:8
  520.3 34.2 %collective-permute-done.15 = bf16[2048,384]{1,0:T(8,128)(2,1)S(1)} collective-permute-done((bf16[2048,384]{1,0:T(8,128)(2,1)S(1)}, bf16[2048,384]{1,0:T(8,128)(2,1)S(1)}, u32[]{:S(2)}, u32[]{:S(2)}) %collective-permute-start.15) | collective-permute-done | bytes 1572896 | tf_op jit(solution)/shard_map/ppermute | solution.py:8
  554.5 7.2 %maximum_select_fusion.11 = bf16[4096,384]{1,0:T(8,128)(2,1)S(1)} fusion(bf16[2048,384]{1,0:T(8,128)(2,1)S(1)} %maximum_select_fusion.14, bf16[2048,384]{1,0:T(8,128)(2,1)S(1)} %collective-permute-done.15, pred[]{:T(512)S(6)} %eq.15), kind=kLoop, calls=%fused_computation.41 | loop fusion | flops 14155776 | bytes 6291457 | tf_op jit(solution)/shard_map/jit(_where)/select_n | solution.py:37
  563.9 66.9 %collective-permute-done.16 = bf16[4096,384]{1,0:T(8,128)(2,1)S(1)} collective-permute-done((bf16[4096,384]{1,0:T(8,128)(2,1)S(1)}, bf16[4096,384]{1,0:T(8,128)(2,1)S(1)}, u32[]{:S(2)}, u32[]{:S(2)}) %collective-permute-start.16) | collective-permute-done | bytes 3145760 | tf_op jit(solution)/shard_map/ppermute | solution.py:8
  637.0 5.1 collective-permute-done.17
  (86 shorter events, 65.9 us)
Async XLA Ops:
  0.6 293.9 %copy-start = (bf16[128,8192]{1,0:T(8,128)(2,1)S(1)}, bf16[128,8192]{1,0:T(8,128)(2,1)}, u32[]{:S(2)}) copy-start(bf16[128,8192]{1,0:T(8,128)(2,1)} %param.20) | copy-start | bytes 6291460
  48.8 3.8 collective-permute-start
  58.0 70.5 %collective-permute-start.1 = (bf16[4096,384]{1,0:T(8,128)(2,1)}, bf16[4096,384]{1,0:T(8,128)(2,1)}, u32[]{:S(2)}, u32[]{:S(2)}) collective-permute-start(bf16[4096,384]{1,0:T(8,128)(2,1)} %maximum_select_fusion.8), channel_id=1, source_target_pairs={{0,16},{8,24},{16,0},{24,8},{32,48},{40,56},{48,32},{56,40},{64,80... | collective-permute-start | bytes 9437192 | tf_op jit(solution)/shard_map/ppermute | solution.py:8
  137.5 11.9 %collective-permute-start.2 = (f32[256,384]{0,1:T(8,128)S(1)}, f32[256,384]{0,1:T(8,128)S(1)}, u32[]{:S(2)}, u32[]{:S(2)}) collective-permute-start(f32[256,384]{0,1:T(8,128)S(1)} %fusion.28), channel_id=1, source_target_pairs={{0,32},{8,40},{16,48},{24,56},{32,0},{40,8},{48,16},{56,24},{64,96... | collective-permute-start | bytes 1179656 | tf_op jit(solution)/shard_map/ppermute | solution.py:8
  175.9 2.3 collective-permute-start.3
  178.6 36.5 %collective-permute-start.4 = (bf16[2048,384]{1,0:T(8,128)(2,1)S(1)}, bf16[2048,384]{1,0:T(8,128)(2,1)S(1)}, u32[]{:S(2)}, u32[]{:S(2)}) collective-permute-start(bf16[2048,384]{1,0:T(8,128)(2,1)S(1)} %maximum_select_fusion.12), channel_id=1, source_target_pairs={{0,16},{8,24},{16,0},{24,8},{32,48},{40,56},{48,32},{56,40},{64,80... | collective-permute-start | bytes 4718600 | tf_op jit(solution)/shard_map/ppermute | solution.py:8
  223.4 71.1 %collective-permute-start.5 = (bf16[4096,384]{1,0:T(8,128)(2,1)}, bf16[4096,384]{1,0:T(8,128)(2,1)}, u32[]{:S(2)}, u32[]{:S(2)}) collective-permute-start(bf16[4096,384]{1,0:T(8,128)(2,1)} %maximum_select_fusion.9), channel_id=1, source_target_pairs={{0,32},{8,40},{16,48},{24,56},{32,0},{40,8},{48,16},{56,24},{64,96... | collective-permute-start | bytes 9437192 | tf_op jit(solution)/shard_map/ppermute | solution.py:8
  300.9 5.9 collective-permute-start.6
  323.1 1.7 collective-permute-start.7
  325.2 19.7 %collective-permute-start.8 = (bf16[1024,384]{1,0:T(8,128)(2,1)S(1)}, bf16[1024,384]{1,0:T(8,128)(2,1)S(1)}, u32[]{:S(2)}, u32[]{:S(2)}) collective-permute-start(bf16[1024,384]{1,0:T(8,128)(2,1)S(1)} %maximum_select_fusion.21), channel_id=1, source_target_pairs={{0,16},{8,24},{16,0},{24,8},{32,48},{40,56},{48,32},{56,40},{64,80... | collective-permute-start | bytes 2359304 | tf_op jit(solution)/shard_map/ppermute | solution.py:8
  345.3 114.2 %copy-start.6 = (bf16[64,8192]{1,0:T(8,128)(2,1)S(1)}, bf16[64,8192]{1,0:T(8,128)(2,1)}, u32[]{:S(2)}) copy-start(bf16[64,8192]{1,0:T(8,128)(2,1)} %param.21) | copy-start | bytes 3145732
  345.3 37.2 %collective-permute-start.9 = (bf16[2048,384]{1,0:T(8,128)(2,1)S(1)}, bf16[2048,384]{1,0:T(8,128)(2,1)S(1)}, u32[]{:S(2)}, u32[]{:S(2)}) collective-permute-start(bf16[2048,384]{1,0:T(8,128)(2,1)S(1)} %maximum_select_fusion.13), channel_id=1, source_target_pairs={{0,32},{8,40},{16,48},{24,56},{32,0},{40,8},{48,16},{56,24},{64,96... | collective-permute-start | bytes 4718600 | tf_op jit(solution)/shard_map/ppermute | solution.py:8
  390.7 68.7 %collective-permute-start.10 = (bf16[4096,384]{1,0:T(8,128)(2,1)}, bf16[4096,384]{1,0:T(8,128)(2,1)}, u32[]{:S(2)}, u32[]{:S(2)}) collective-permute-start(bf16[4096,384]{1,0:T(8,128)(2,1)} %maximum_select_fusion.10), channel_id=1, source_target_pairs={{0,64},{8,72},{16,80},{24,88},{32,96},{40,104},{48,112},{56,120},{... | collective-permute-start | bytes 9437192 | tf_op jit(solution)/shard_map/ppermute | solution.py:8
  465.6 6.2 collective-permute-start.11
  485.6 1.4 collective-permute-start.12
  487.2 11.2 %collective-permute-start.13 = (bf16[512,384]{1,0:T(8,128)(2,1)S(1)}, bf16[512,384]{1,0:T(8,128)(2,1)S(1)}, u32[]{:S(2)}, u32[]{:S(2)}) collective-permute-start(bf16[512,384]{1,0:T(8,128)(2,1)S(1)} %maximum_select_fusion.23), channel_id=1, source_target_pairs={{0,16},{8,24},{16,0},{24,8},{32,48},{40,56},{48,32},{56,40},{64,80... | collective-permute-start | bytes 1179656 | tf_op jit(solution)/shard_map/ppermute | solution.py:8
  498.7 20.3 %collective-permute-start.14 = (bf16[1024,384]{1,0:T(8,128)(2,1)S(1)}, bf16[1024,384]{1,0:T(8,128)(2,1)S(1)}, u32[]{:S(2)}, u32[]{:S(2)}) collective-permute-start(bf16[1024,384]{1,0:T(8,128)(2,1)S(1)} %maximum_select_fusion.22), channel_id=1, source_target_pairs={{0,32},{8,40},{16,48},{24,56},{32,0},{40,8},{48,16},{56,24},{64,96... | collective-permute-start | bytes 2359304 | tf_op jit(solution)/shard_map/ppermute | solution.py:8
  519.5 111.3 %copy-start.7 = (bf16[32,8192]{1,0:T(8,128)(2,1)S(1)}, bf16[32,8192]{1,0:T(8,128)(2,1)}, u32[]{:S(2)}) copy-start(bf16[32,8192]{1,0:T(8,128)(2,1)} %param.22) | copy-start | bytes 1572868
  519.5 35.0 %collective-permute-start.15 = (bf16[2048,384]{1,0:T(8,128)(2,1)S(1)}, bf16[2048,384]{1,0:T(8,128)(2,1)S(1)}, u32[]{:S(2)}, u32[]{:S(2)}) collective-permute-start(bf16[2048,384]{1,0:T(8,128)(2,1)S(1)} %maximum_select_fusion.14), channel_id=1, source_target_pairs={{0,64},{8,72},{16,80},{24,88},{32,96},{40,104},{48,112},{56,120},{... | collective-permute-start | bytes 4718600 | tf_op jit(solution)/shard_map/ppermute | solution.py:8
  561.7 69.1 %collective-permute-start.16 = (bf16[4096,384]{1,0:T(8,128)(2,1)S(1)}, bf16[4096,384]{1,0:T(8,128)(2,1)S(1)}, u32[]{:S(2)}, u32[]{:S(2)}) collective-permute-start(bf16[4096,384]{1,0:T(8,128)(2,1)S(1)} %maximum_select_fusion.11), channel_id=1, source_target_pairs={{0,128},{8,136},{16,144},{24,152},{32,160},{40,168},{48,176},{56,1... | collective-permute-start | bytes 9437192 | tf_op jit(solution)/shard_map/ppermute | solution.py:8
  632.6 4.3 collective-permute-start.18
  634.6 7.5 %collective-permute-start.17 = (f32[2,1,16,384]{3,2,1,0:T(8,128)S(1)}, f32[2,1,16,384]{3,2,1,0:T(8,128)S(1)}, u32[]{:S(2)}, u32[]{:S(2)}) collective-permute-start(f32[2,1,16,384]{3,2,1,0:T(8,128)S(1)} %get-tuple-element.27), channel_id=1, source_target_pairs={{0,8},{8,16},{16,24},{24,32},{32,40},{40,48},{48,56},{56,64},{64,7... | collective-permute-start | bytes 147464 | tf_op jit(solution)/shard_map/ppermute | solution.py:19
  642.1 5.9 collective-permute-start.20
  645.5 5.6 collective-permute-start.19
  (5 other events, 188.6 us)
